TPU v7x, 128 devices: a whole 4x4x4 slice. The times are simulated.
128 devices in a mesh: row: 16 (over z_lo, x, core), col: 8 (over y, z_hi).
Axes of the slice: x: 4, y: 4, z: 4 (z_hi: 2, z_lo: 2; z = z_hi * 2 + z_lo), core: 2. Of those that a mesh axis runs over, the one named last changes fastest.
Arguments:
- slab_embed: float32 [65536, 768], P(('col', 'row')), may hold values from -1 to 1
- coverage_old: float32 [65536], P('col'), may hold values from 2 to 4.5
- sel_index: int32 [2048], P('row'), may hold values from 0 to 65535
- cand_index: int32 [3072], P('row'), may hold values from 0 to 65535
Outputs:
- coverage: float32 [65536], P('col')
- total_gain: float32 [3072], P('row')
Inputs may be any that keep to these rules, and one draw needn't show every extreme that they name: `sel_index`: indices into the slab. `cand_index`: indices into the slab.
All inputs are finite; a program needn't handle non-finite values.
Results may differ from a plain program's by a relative error of at most 0.00014.
Values sent between devices are 32-bit elements; how exact they have to be, the bound alone decides.
No kernel may reach another device: no remote copies, remote signals or barrier semaphores. Data moves between devices by JAX's collectives and lax.ppermute only.
A program may use at most 128 MiB of HBM per device.

v0:
```python
import jax
import jax.numpy as jnp
from jax import lax
from jax.sharding import PartitionSpec as P


def similar(left, right):
    return lax.dot_general(
        left,
        right,
        (((1,), (1,)), ((), ())),
        precision=lax.Precision.HIGH,
        preferred_element_type=jnp.float32,
    )


def lookup(source, indices, first_row):
    position = indices - first_row
    inside = (position >= 0) & (position < source.shape[0])
    picked = jnp.take(source, jnp.clip(position, 0, source.shape[0] - 1), axis=0)
    return jnp.where(inside[:, None], picked, 0.0)


def shift(value, axis, size, pairs):
    return lax.ppermute(value, axis, [(i, j) for i, j in pairs if i < size and j < size])


def col_parts(value, n_y, n_z):
    size = n_y * n_z
    here = lax.axis_index("col")
    y, z = (here // n_z, here % n_z)
    if n_z == 2:
        other = shift(value, "col", size, [(c, c ^ 1) for c in range(size)])
        pair = jnp.where(z == 0, jnp.stack([value, other]), jnp.stack([other, value]))
    else:
        pair = value[None]
    if n_y == 1:
        return pair
    up = [(c, (c // n_z + 1) % n_y * n_z + c % n_z) for c in range(size)]
    down = [(c, (c // n_z - 1) % n_y * n_z + c % n_z) for c in range(size)]
    from_below = shift(pair, "col", size, up)
    from_above = shift(pair, "col", size, down)
    parts = [pair, from_above, None, from_below]
    if n_y == 4:
        parts[2] = shift(from_below, "col", size, up)
        ordered = jnp.stack(parts)
    else:
        ordered = jnp.stack([pair, from_above])
    return jnp.roll(ordered, y, axis=0).reshape((size,) + value.shape)


def col_masked_sum(value, n_y, n_z):
    size = n_y * n_z
    if n_z == 2:
        value = value + shift(value, "col", size, [(c, c ^ 1) for c in range(size)])
    up = [(c, (c // n_z + 1) % n_y * n_z + c % n_z) for c in range(size)]
    down = [(c, (c // n_z - 1) % n_y * n_z + c % n_z) for c in range(size)]
    from_below = shift(value, "col", size, up)
    from_above = shift(value, "col", size, down)
    far = shift(from_below, "col", size, up)
    return value + from_below + from_above + far


def row_max(value, n):
    here = lax.axis_index("row")
    value = jnp.maximum(value, shift(value, "row", n, [(r, r ^ 1) for r in range(n)]))
    x_up = [(r, r & ~6 | ((r >> 1 & 3) + 1) % 4 << 1) for r in range(n)]
    x_down = [(r, r & ~6 | ((r >> 1 & 3) - 1) % 4 << 1) for r in range(n)]
    value = jnp.maximum(
        value, jnp.maximum(shift(value, "row", n, x_up), shift(value, "row", n, x_down))
    )
    value = jnp.maximum(value, shift(value, "row", n, x_up))
    value = jnp.maximum(value, shift(value, "row", n, [(r, r ^ 8) for r in range(n)]))
    return value


def body(slab_embed, coverage_old, sel_index, cand_index):
    col_id = lax.axis_index("col")
    gathered = lax.all_gather(slab_embed, "row", axis=0, tiled=True)
    first_row = col_id * gathered.shape[0]
    n_sel = sel_index.shape[0]
    picked = col_masked_sum(
        jnp.concatenate(
            [lookup(gathered, sel_index, first_row), lookup(gathered, cand_index, first_row)]
        ),
        4,
        2,
    )
    selected, chosen = (picked[:n_sel], picked[n_sel:])
    partial_value = jnp.max(similar(selected, gathered), axis=0)
    reached = row_max(partial_value, 16)
    coverage = jnp.maximum(coverage_old, reached)
    gain_part = jnp.sum(jnp.maximum(similar(chosen, gathered) - coverage[None, :], 0.0), axis=1)
    total_gain = jnp.sum(col_parts(gain_part, 4, 2), axis=0)
    return (coverage, total_gain)


def solution(mesh):
    in_specs = (P(("col", "row"), None), P("col"), P("row"), P("row"))
    out_specs = (P("col"), P("row"))
    return jax.shard_map(body, mesh=mesh, in_specs=in_specs, out_specs=out_specs, check_vma=False)
```

profile of v0, /device:TPU:0, one launch (start us, length us, event | category | flops | bytes accessed | tf_op | source)
XLA Modules:
  0.0 307.7 jit_solution(16716492885634201981)
XLA Ops:
  7.2 0.0 all-gather.2.cloned.1.call-start
  7.2 0.7 all-gather.2.cloned.1.call-update
  7.9 0.7 compare_and_fusion
  8.6 0.7 compare_and_fusion.2
  9.3 134.1 %all-gather.2.cloned.1.call-done = f32[8192,768]{1,0:T(8,128)} async-done(((f32[512,768]{1,0:T(8,128)}), f32[8192,768]{1,0:T(8,128)}) %all-gather.2.cloned.1.call-update) | async-done | bytes 25165840 | tf_op jit(solution)/shard_map/all_gather | solution.py:79
  143.4 9.3 %gather_fusion.1 = f32[192,768]{1,0:T(8,128)S(1)} fusion(f32[8192,768]{1,0:T(8,128)} %all-gather.2.cloned.1.call-done, s32[1024]{0:T(1024)S(1)} %pad_clamp_fusion), kind=kCustom, calls=%fused_computation.1 | custom fusion | bytes 1180416 | tf_op jit(solution)/shard_map/jit(_take)/gather | solution.py:20
  152.7 0.0 copy-start.1
  152.7 0.1 select_select_fusion
  152.9 9.1 %gather_fusion = f32[128,768]{1,0:T(8,128)S(1)} fusion(f32[8192,768]{1,0:T(8,128)} %all-gather.2.cloned.1.call-done, s32[1024]{0:T(1024)S(1)} %pad_clamp_fusion.1), kind=kCustom, calls=%fused_computation | custom fusion | bytes 786944 | tf_op jit(solution)/shard_map/jit(_take)/gather | solution.py:20
  162.0 0.1 select_select_fusion.1
  162.1 0.1 pad_maximum_fusion
  162.2 2.9 collective-permute-start
  165.1 22.6 %collective-permute-done = f32[320,768]{1,0:T(8,128)S(1)} collective-permute-done((f32[320,768]{1,0:T(8,128)S(1)}, f32[320,768]{1,0:T(8,128)S(1)}, u32[]{:S(2)}, u32[]{:S(2)}) %collective-permute-start) | collective-permute-done | bytes 983072 | tf_op jit(solution)/shard_map/ppermute | solution.py:25
  187.7 0.1 fusion.4
  187.8 1.6 collective-permute-start.1
  189.4 1.8 collective-permute-start.2
  191.1 21.1 %collective-permute-done.1 = f32[320,768]{1,0:T(8,128)S(1)} collective-permute-done((f32[320,768]{1,0:T(8,128)S(1)}, f32[320,768]{1,0:T(8,128)S(1)}, u32[]{:S(2)}, u32[]{:S(2)}) %collective-permute-start.1) | collective-permute-done | bytes 983072 | tf_op jit(solution)/shard_map/ppermute | solution.py:25
  212.2 0.3 collective-permute-start.3
  212.5 0.0 collective-permute-done.2
  212.5 23.1 %collective-permute-done.3 = f32[320,768]{1,0:T(8,128)S(1)} collective-permute-done((f32[320,768]{1,0:T(8,128)S(1)}, f32[320,768]{1,0:T(8,128)S(1)}, u32[]{:S(2)}, u32[]{:S(2)}) %collective-permute-start.3) | collective-permute-done | bytes 983072 | tf_op jit(solution)/shard_map/ppermute | solution.py:25
  235.6 0.3 add_add_fusion
  235.9 16.5 %convolution_reduce_fusion = f32[8192]{0:T(1024)S(1)} fusion(f32[8192,768]{1,0:T(8,128)} %all-gather.2.cloned.1.call-done, f32[320,768]{1,0:T(8,128)S(1)} %add_add_fusion), kind=kOutput, calls=%fused_computation.5 | convolution fusion | flops 4832878592 | bytes 25591808 | tf_op jit(solution)/shard_map/dot_general | solution.py:8
  252.4 0.1 collective-permute-start.4
  252.5 1.2 collective-permute-done.4
  253.7 1.1 collective-permute-start.5
  254.8 2.1 collective-permute-start.6
  256.9 1.9 collective-permute-done.5
  258.8 0.0 collective-permute-done.6
  258.8 1.1 collective-permute-start.7
  260.0 4.1 %collective-permute-done.7 = f32[8192]{0:T(1024)S(1)} collective-permute-done((f32[8192]{0:T(1024)S(1)}, f32[8192]{0:T(1024)S(1)}, u32[]{:S(2)}, u32[]{:S(2)}) %collective-permute-start.7) | collective-permute-done | bytes 32800 | tf_op jit(solution)/shard_map/ppermute | solution.py:25
  264.0 1.7 collective-permute-start.8
  265.8 2.2 collective-permute-done.8
  268.0 0.0 copy-done.1
  268.0 0.0 copy-start
  268.0 17.4 %fusion.1 = f32[192]{0:T(256)S(1)} fusion(f32[8192]{0:T(1024)S(1)} %maximum_maximum_fusion, f32[8192,768]{1,0:T(8,128)} %all-gather.2.cloned.1.call-done, f32[320,768]{1,0:T(8,128)S(1)} %add_add_fusion), kind=kOutput, calls=%fused_computation.4 | convolution fusion | flops 7252475904 | bytes 25789184 | tf_op jit(solution)/shard_map/dot_general | solution.py:8
  285.4 3.1 %collective-permute-start.9 = (f32[192]{0:T(256)S(1)}, f32[192]{0:T(256)S(1)}, u32[]{:S(2)}, u32[]{:S(2)}) collective-permute-start(f32[192]{0:T(256)S(1)} %fusion.1), channel_id=1, source_target_pairs={{0,1},{1,0},{2,3},{3,2},{4,5},{5,4},{6,7},{7,6},{8,9},{9,8},{10,11... | collective-permute-start | bytes 2312 | tf_op jit(solution)/shard_map/ppermute | solution.py:25
  288.5 2.0 collective-permute-done.9
  290.5 0.1 collective-permute-start.11
  290.7 3.2 %collective-permute-start.10 = (f32[2,192]{1,0:T(2,128)S(1)}, f32[2,192]{1,0:T(2,128)S(1)}, u32[]{:S(2)}, u32[]{:S(2)}) collective-permute-start(f32[2,192]{1,0:T(2,128)S(1)} %maximum_select_fusion), channel_id=1, source_target_pairs={{0,6},{1,7},{2,0},{3,1},{4,2},{5,3},{6,4},{7,5},{8,14},{9,15},{10,... | collective-permute-start | bytes 4616 | tf_op jit(solution)/shard_map/ppermute | solution.py:25
  293.8 1.6 collective-permute-done.11
  295.4 0.0 collective-permute-start.12
  295.4 0.0 collective-permute-done.10
  295.5 4.8 %collective-permute-done.12 = f32[2,192]{1,0:T(2,128)S(1)} collective-permute-done((f32[2,192]{1,0:T(2,128)S(1)}, f32[2,192]{1,0:T(2,128)S(1)}, u32[]{:S(2)}, u32[]{:S(2)}) %collective-permute-start.12) | collective-permute-done | bytes 1568 | tf_op jit(solution)/shard_map/ppermute | solution.py:25
  300.2 0.6 dynamic-slice_reduce_fusion
  300.8 0.0 copy-done
  (12 shorter events, 0.1 us)
Async XLA Ops:
  7.2 136.2 %all-gather.2.cloned.1.call-start = ((), (), s32[]{:S(2)}) async-start(), calls=%async_computation | async-start | bytes 26738688 | tf_op jit(solution)/shard_map/all_gather | solution.py:79
  152.7 115.2 %copy-start.1 = (f32[8192]{0:T(1024)S(1)}, f32[8192]{0:T(1024)}, u32[]{:S(2)}) copy-start(f32[8192]{0:T(1024)} %param.5) | copy-start | bytes 98308
  162.2 25.5 %collective-permute-start = (f32[320,768]{1,0:T(8,128)S(1)}, f32[320,768]{1,0:T(8,128)S(1)}, u32[]{:S(2)}, u32[]{:S(2)}) collective-permute-start(f32[320,768]{1,0:T(8,128)S(1)} %pad_maximum_fusion), channel_id=1, source_target_pairs={{0,1},{1,0},{2,3},{3,2},{4,5},{5,4},{6,7},{7,6},{8,9},{9,8},{10,11... | collective-permute-start | bytes 2949128 | tf_op jit(solution)/shard_map/ppermute | solution.py:25
  187.8 24.4 %collective-permute-start.1 = (f32[320,768]{1,0:T(8,128)S(1)}, f32[320,768]{1,0:T(8,128)S(1)}, u32[]{:S(2)}, u32[]{:S(2)}) collective-permute-start(f32[320,768]{1,0:T(8,128)S(1)} %fusion.4), channel_id=1, source_target_pairs={{0,2},{1,3},{2,4},{3,5},{4,6},{5,7},{6,0},{7,1},{8,10},{9,11},{10,... | collective-permute-start | bytes 2949128 | tf_op jit(solution)/shard_map/ppermute | solution.py:25
  189.4 23.1 %collective-permute-start.2 = (f32[320,768]{1,0:T(8,128)S(1)}, f32[320,768]{1,0:T(8,128)S(1)}, u32[]{:S(2)}, u32[]{:S(2)}) collective-permute-start(f32[320,768]{1,0:T(8,128)S(1)} %fusion.4), channel_id=1, source_target_pairs={{0,6},{1,7},{2,0},{3,1},{4,2},{5,3},{6,4},{7,5},{8,14},{9,15},{10,... | collective-permute-start | bytes 2949128 | tf_op jit(solution)/shard_map/ppermute | solution.py:25
  212.2 23.4 %collective-permute-start.3 = (f32[320,768]{1,0:T(8,128)S(1)}, f32[320,768]{1,0:T(8,128)S(1)}, u32[]{:S(2)}, u32[]{:S(2)}) collective-permute-start(f32[320,768]{1,0:T(8,128)S(1)} %collective-permute-done.1), channel_id=1, source_target_pairs={{0,2},{1,3},{2,4},{3,5},{4,6},{5,7},{6,0},{7,1},{8,10},{9,11},{10,... | collective-permute-start | bytes 2949128 | tf_op jit(solution)/shard_map/ppermute | solution.py:25
  252.4 1.3 collective-permute-start.4
  253.7 5.1 %collective-permute-start.5 = (f32[8192]{0:T(1024)S(1)}, f32[8192]{0:T(1024)S(1)}, u32[]{:S(2)}, u32[]{:S(2)}) collective-permute-start(f32[8192]{0:T(1024)S(1)} %max.32), channel_id=1, source_target_pairs={{0,16},{8,24},{16,32},{24,40},{32,48},{40,56},{48,0},{56,8},{64,80... | collective-permute-start | bytes 98312 | tf_op jit(solution)/shard_map/ppermute | solution.py:25
  254.8 4.0 %collective-permute-start.6 = (f32[8192]{0:T(1024)S(1)}, f32[8192]{0:T(1024)S(1)}, u32[]{:S(2)}, u32[]{:S(2)}) collective-permute-start(f32[8192]{0:T(1024)S(1)} %max.32), channel_id=1, source_target_pairs={{0,48},{8,56},{16,0},{24,8},{32,16},{40,24},{48,32},{56,40},{64,11... | collective-permute-start | bytes 98312 | tf_op jit(solution)/shard_map/ppermute | solution.py:25
  258.8 5.2 %collective-permute-start.7 = (f32[8192]{0:T(1024)S(1)}, f32[8192]{0:T(1024)S(1)}, u32[]{:S(2)}, u32[]{:S(2)}) collective-permute-start(f32[8192]{0:T(1024)S(1)} %maximum_maximum_fusion.1), channel_id=1, source_target_pairs={{0,16},{8,24},{16,32},{24,40},{32,48},{40,56},{48,0},{56,8},{64,80... | collective-permute-start | bytes 98312 | tf_op jit(solution)/shard_map/ppermute | solution.py:25
  264.0 3.9 %collective-permute-start.8 = (f32[8192]{0:T(1024)S(1)}, f32[8192]{0:T(1024)S(1)}, u32[]{:S(2)}, u32[]{:S(2)}) collective-permute-start(f32[8192]{0:T(1024)S(1)} %max.35), channel_id=1, source_target_pairs={{0,64},{8,72},{16,80},{24,88},{32,96},{40,104},{48,112},{56,120},{... | collective-permute-start | bytes 98312 | tf_op jit(solution)/shard_map/ppermute | solution.py:25
  268.0 32.9 %copy-start = (f32[8192]{0:T(1024)}, f32[8192]{0:T(1024)S(1)}, u32[]{:S(2)}) copy-start(f32[8192]{0:T(1024)S(1)} %maximum_maximum_fusion) | copy-start | bytes 98308
  285.4 5.2 %collective-permute-start.9 = (f32[192]{0:T(256)S(1)}, f32[192]{0:T(256)S(1)}, u32[]{:S(2)}, u32[]{:S(2)}) collective-permute-start(f32[192]{0:T(256)S(1)} %fusion.1), channel_id=1, source_target_pairs={{0,1},{1,0},{2,3},{3,2},{4,5},{5,4},{6,7},{7,6},{8,9},{9,8},{10,11... | collective-permute-start | bytes 2312 | tf_op jit(solution)/shard_map/ppermute | solution.py:25
  290.5 4.9 %collective-permute-start.11 = (f32[2,192]{1,0:T(2,128)S(1)}, f32[2,192]{1,0:T(2,128)S(1)}, u32[]{:S(2)}, u32[]{:S(2)}) collective-permute-start(f32[2,192]{1,0:T(2,128)S(1)} %maximum_select_fusion), channel_id=1, source_target_pairs={{0,2},{1,3},{2,4},{3,5},{4,6},{5,7},{6,0},{7,1},{8,10},{9,11},{10,... | collective-permute-start | bytes 4616 | tf_op jit(solution)/shard_map/ppermute | solution.py:25
  290.7 4.8 %collective-permute-start.10 = (f32[2,192]{1,0:T(2,128)S(1)}, f32[2,192]{1,0:T(2,128)S(1)}, u32[]{:S(2)}, u32[]{:S(2)}) collective-permute-start(f32[2,192]{1,0:T(2,128)S(1)} %maximum_select_fusion), channel_id=1, source_target_pairs={{0,6},{1,7},{2,0},{3,1},{4,2},{5,3},{6,4},{7,5},{8,14},{9,15},{10,... | collective-permute-start | bytes 4616 | tf_op jit(solution)/shard_map/ppermute | solution.py:25
  295.4 4.8 %collective-permute-start.12 = (f32[2,192]{1,0:T(2,128)S(1)}, f32[2,192]{1,0:T(2,128)S(1)}, u32[]{:S(2)}, u32[]{:S(2)}) collective-permute-start(f32[2,192]{1,0:T(2,128)S(1)} %collective-permute-done.11), channel_id=1, source_target_pairs={{0,2},{1,3},{2,4},{3,5},{4,6},{5,7},{6,0},{7,1},{8,10},{9,11},{10,... | collective-permute-start | bytes 4616 | tf_op jit(solution)/shard_map/ppermute | solution.py:25
Sparse Core Ops, SparseCore 0:
  9.7 133.6 all-gather.1
where the time goes:
time: 308 us
  waiting for transfers between devices  219 us (71%)
  matrix products  33.9 us (11%)
  starting transfers between devices  19.1 us (6%)
  local copies, waits for them, and re-layouts  18.5 us (6%)
  between operations  14.2 us (5%)
    all_gather x1, waiting for transfers between devices, body(): gathered = lax.all_gather(slab_embed, 'row', axis=0, tiled=True)  134 us
    ppermute x13, waiting for transfers between devices, shift(): lax.ppermute(value, axis, [(i, j) for i, j in pairs if i < size and j < s...  84.5 us
    dot_general x2, matrix products, similar(): lax.dot_general(left, right, (((1,), (1,)), ((), ())), precision=lax.Prec...  33.9 us
    ppermute x13, starting transfers between devices, shift(): lax.ppermute(value, axis, [(i, j) for i, j in pairs if i < size and j < s...  19.1 us
    gather x2, local copies, waits for them, and re-layouts, lookup(): jnp.take(source, jnp.clip(position, 0, source.shape[0] - 1), axis=0)  18.5 us
  transfers between devices with their start and end apart: 14, of which 11 were waited for; matrix products, arithmetic and copies ran while one was open for 0% of the time, Pallas kernels for 0%

commit v1 on v0

--- a/solution.py
+++ b/solution.py
@@ -76,7 +76,9 @@
 
 def body(slab_embed, coverage_old, sel_index, cand_index):
     col_id = lax.axis_index("col")
-    gathered = lax.all_gather(slab_embed, "row", axis=0, tiled=True)
+    gathered = jnp.concatenate(
+        lax.all_to_all(jnp.stack([slab_embed] * lax.axis_size("row")), "row", 0, 0), axis=0
+    )
     first_row = col_id * gathered.shape[0]
     n_sel = sel_index.shape[0]
     picked = col_masked_sum(

time: 308 us -> 514 us (1.67)
  waiting for transfers between devices: 219 us -> 425 us
  between operations: 14.2 us -> 0.86 us
  local copies, waits for them, and re-layouts: 18.5 us -> 30.7 us
    all_to_all x0 -> x1, waiting for transfers between devices: none -> 337 us  [body(): lax.all_to_all(jnp.stack([slab_embed] * lax.axis_size('row')), 'row', 0, 0)]
    all_gather x1 -> x0, waiting for transfers between devices: 134 us -> none  [body(): gathered = lax.all_gather(slab_embed, 'row', axis=0, tiled=True)]
    another operation x0 -> x1, local copies, waits for them, and re-layouts: none -> 12.1 us  [body(): jnp.stack([slab_embed] * lax.axis_size('row'))]
    all_to_all x0 -> x1, starting transfers between devices: none -> 6.02 us  [body(): lax.all_to_all(jnp.stack([slab_embed] * lax.axis_size('row')), 'row', 0, 0)]
  transfers between devices with their start and end apart: 14 -> 14, of which waited for: 11 -> 12; matrix products, arithmetic and copies ran while one was open for 0% -> 0% of each run, Pallas kernels for 0% -> 0%
where the time goes in v1:
time: 514 us
  waiting for transfers between devices  425 us (83%)
  matrix products  33.9 us (7%)
  local copies, waits for them, and re-layouts  30.7 us (6%)
  starting transfers between devices  22.7 us (4%)
    all_to_all x1, waiting for transfers between devices, body(): lax.all_to_all(jnp.stack([slab_embed] * lax.axis_size('row')), 'row', 0, 0)  337 us
    ppermute x13, waiting for transfers between devices, shift(): lax.ppermute(value, axis, [(i, j) for i, j in pairs if i < size and j < s...  88 us
    dot_general x2, matrix products, similar(): lax.dot_general(left, right, (((1,), (1,)), ((), ())), precision=lax.Prec...  33.9 us
    gather x2, local copies, waits for them, and re-layouts, lookup(): jnp.take(source, jnp.clip(position, 0, source.shape[0] - 1), axis=0)  18.5 us
    ppermute x13, starting transfers between devices, shift(): lax.ppermute(value, axis, [(i, j) for i, j in pairs if i < size and j < s...  16.7 us
    another operation x1, local copies, waits for them, and re-layouts, body(): jnp.stack([slab_embed] * lax.axis_size('row'))  12.1 us
  transfers between devices with their start and end apart: 14, of which 12 were waited for; matrix products, arithmetic and copies ran while one was open for 0% of the time, Pallas kernels for 0%

profile of v1, /device:TPU:0, one launch (start us, length us, event | category | flops | bytes accessed | tf_op | source)
XLA Modules:
  0.0 514.2 jit_solution(3262516847430330431)
XLA Ops:
  0.6 12.1 %stack.24 = f32[16,512,768]{2,1,0:T(8,128)} broadcast(f32[512,768]{1,0:T(8,128)} %param.4), dimensions={1,2} | broadcast | bytes 26738688 | tf_op jit(solution)/shard_map/stack | solution.py:80
  12.8 0.0 copy-start.2
  12.8 0.0 copy-start.3
  12.8 6.0 %all-to-all-start = ((f32[16,512,768]{2,1,0:T(8,128)}), f32[16,512,768]{2,1,0:T(8,128)}, u32[]{:S(2)}, u32[]{:S(2)}) async-start(f32[16,512,768]{2,1,0:T(8,128)} %stack.24), calls=%async_computation | async-start | bytes 50331648 | tf_op jit(solution)/shard_map/all_to_all | solution.py:80
  18.8 0.0 copy-done.2
  18.8 0.0 copy-done.3
  18.9 336.7 %all-to-all-done = f32[16,512,768]{2,1,0:T(8,128)} async-done(((f32[16,512,768]{2,1,0:T(8,128)}), f32[16,512,768]{2,1,0:T(8,128)}, u32[]{:S(2)}, u32[]{:S(2)}) %all-to-all-start) | async-done | bytes 25165856 | tf_op jit(solution)/shard_map/all_to_all | solution.py:80
  355.6 9.3 %gather_fusion.1 = f32[192,768]{1,0:T(8,128)S(1)} fusion(f32[8192,768]{1,0:T(8,128)} %bitcast, s32[1024]{0:T(1024)S(1)} %pad_clamp_fusion), kind=kCustom, calls=%fused_computation.1 | custom fusion | bytes 1180416 | tf_op jit(solution)/shard_map/jit(_take)/gather | solution.py:20
  365.0 0.0 copy-start.1
  365.0 9.1 %gather_fusion = f32[128,768]{1,0:T(8,128)S(1)} fusion(f32[8192,768]{1,0:T(8,128)} %bitcast, s32[1024]{0:T(1024)S(1)} %pad_clamp_fusion.1), kind=kCustom, calls=%fused_computation | custom fusion | bytes 786944 | tf_op jit(solution)/shard_map/jit(_take)/gather | solution.py:20
  374.1 0.1 select_select_fusion
  374.3 0.1 select_select_fusion.1
  374.4 0.1 pad_maximum_fusion
  374.5 3.7 collective-permute-start
  378.1 21.8 %collective-permute-done = f32[320,768]{1,0:T(8,128)S(1)} collective-permute-done((f32[320,768]{1,0:T(8,128)S(1)}, f32[320,768]{1,0:T(8,128)S(1)}, u32[]{:S(2)}, u32[]{:S(2)}) %collective-permute-start) | collective-permute-done | bytes 983072 | tf_op jit(solution)/shard_map/ppermute | solution.py:25
  400.0 0.1 fusion.4
  400.1 1.6 collective-permute-start.1
  401.7 1.7 collective-permute-start.2
  403.4 21.1 %collective-permute-done.1 = f32[320,768]{1,0:T(8,128)S(1)} collective-permute-done((f32[320,768]{1,0:T(8,128)S(1)}, f32[320,768]{1,0:T(8,128)S(1)}, u32[]{:S(2)}, u32[]{:S(2)}) %collective-permute-start.1) | collective-permute-done | bytes 983072 | tf_op jit(solution)/shard_map/ppermute | solution.py:25
  424.4 0.3 collective-permute-start.3
  424.7 0.0 collective-permute-done.2
  424.7 23.1 %collective-permute-done.3 = f32[320,768]{1,0:T(8,128)S(1)} collective-permute-done((f32[320,768]{1,0:T(8,128)S(1)}, f32[320,768]{1,0:T(8,128)S(1)}, u32[]{:S(2)}, u32[]{:S(2)}) %collective-permute-start.3) | collective-permute-done | bytes 983072 | tf_op jit(solution)/shard_map/ppermute | solution.py:25
  447.8 0.2 add_add_fusion
  448.1 16.5 %convolution_reduce_fusion = f32[8192]{0:T(1024)S(1)} fusion(f32[8192,768]{1,0:T(8,128)} %bitcast, f32[320,768]{1,0:T(8,128)S(1)} %add_add_fusion), kind=kOutput, calls=%fused_computation.5 | convolution fusion | flops 4832878592 | bytes 25591808 | tf_op jit(solution)/shard_map/dot_general | solution.py:8
  464.5 0.1 collective-permute-start.4
  464.6 1.2 collective-permute-done.4
  465.8 2.5 collective-permute-start.5
  468.3 0.8 collective-permute-start.6
  469.1 1.9 collective-permute-done.5
  471.0 1.3 collective-permute-done.6
  472.2 0.1 collective-permute-start.7
  472.4 5.0 collective-permute-done.7
  477.4 0.0 collective-permute-start.8
  477.4 3.9 collective-permute-done.8
  481.3 0.0 copy-done.1
  481.4 0.0 copy-start
  481.4 17.4 %fusion.1 = f32[192]{0:T(256)S(1)} fusion(f32[8192]{0:T(1024)S(1)} %maximum_maximum_fusion, f32[8192,768]{1,0:T(8,128)} %bitcast, f32[320,768]{1,0:T(8,128)S(1)} %add_add_fusion), kind=kOutput, calls=%fused_computation.4 | convolution fusion | flops 7252475904 | bytes 25789184 | tf_op jit(solution)/shard_map/dot_general | solution.py:8
  498.8 2.7 collective-permute-start.9
  501.4 2.5 collective-permute-done.9
  503.9 0.1 collective-permute-start.11
  504.0 3.2 collective-permute-start.10
  507.2 1.6 collective-permute-done.11
  508.8 0.0 collective-permute-start.12
  508.8 0.0 collective-permute-done.10
  508.8 4.8 collective-permute-done.12
  513.6 0.6 dynamic-slice_reduce_fusion
  514.2 0.0 copy-done
  (14 shorter events, 0.1 us)
Async XLA Ops:
  12.8 6.0 %copy-start.2 = (s32[192]{0:T(256)S(1)}, s32[192]{0:T(256)}, u32[]{:S(2)}) copy-start(s32[192]{0:T(256)} %param.7) | copy-start | bytes 2308
  12.8 6.1 %copy-start.3 = (s32[128]{0:T(128)S(1)}, s32[128]{0:T(128)}, u32[]{:S(2)}) copy-start(s32[128]{0:T(128)} %param.6) | copy-start | bytes 1540
  12.8 342.9 %all-to-all-start = ((f32[16,512,768]{2,1,0:T(8,128)}), f32[16,512,768]{2,1,0:T(8,128)}, u32[]{:S(2)}, u32[]{:S(2)}) async-start(f32[16,512,768]{2,1,0:T(8,128)} %stack.24), calls=%async_computation | async-start | bytes 50331648 | tf_op jit(solution)/shard_map/all_to_all | solution.py:80
  365.0 116.4 %copy-start.1 = (f32[8192]{0:T(1024)S(1)}, f32[8192]{0:T(1024)}, u32[]{:S(2)}) copy-start(f32[8192]{0:T(1024)} %param.5) | copy-start | bytes 98308
  374.5 25.5 %collective-permute-start = (f32[320,768]{1,0:T(8,128)S(1)}, f32[320,768]{1,0:T(8,128)S(1)}, u32[]{:S(2)}, u32[]{:S(2)}) collective-permute-start(f32[320,768]{1,0:T(8,128)S(1)} %pad_maximum_fusion), channel_id=1, source_target_pairs={{0,1},{1,0},{2,3},{3,2},{4,5},{5,4},{6,7},{7,6},{8,9},{9,8},{10,11... | collective-permute-start | bytes 2949128 | tf_op jit(solution)/shard_map/ppermute | solution.py:25
  400.1 24.4 %collective-permute-start.1 = (f32[320,768]{1,0:T(8,128)S(1)}, f32[320,768]{1,0:T(8,128)S(1)}, u32[]{:S(2)}, u32[]{:S(2)}) collective-permute-start(f32[320,768]{1,0:T(8,128)S(1)} %fusion.4), channel_id=1, source_target_pairs={{0,2},{1,3},{2,4},{3,5},{4,6},{5,7},{6,0},{7,1},{8,10},{9,11},{10,... | collective-permute-start | bytes 2949128 | tf_op jit(solution)/shard_map/ppermute | solution.py:25
  401.7 23.0 %collective-permute-start.2 = (f32[320,768]{1,0:T(8,128)S(1)}, f32[320,768]{1,0:T(8,128)S(1)}, u32[]{:S(2)}, u32[]{:S(2)}) collective-permute-start(f32[320,768]{1,0:T(8,128)S(1)} %fusion.4), channel_id=1, source_target_pairs={{0,6},{1,7},{2,0},{3,1},{4,2},{5,3},{6,4},{7,5},{8,14},{9,15},{10,... | collective-permute-start | bytes 2949128 | tf_op jit(solution)/shard_map/ppermute | solution.py:25
  424.4 23.4 %collective-permute-start.3 = (f32[320,768]{1,0:T(8,128)S(1)}, f32[320,768]{1,0:T(8,128)S(1)}, u32[]{:S(2)}, u32[]{:S(2)}) collective-permute-start(f32[320,768]{1,0:T(8,128)S(1)} %collective-permute-done.1), channel_id=1, source_target_pairs={{0,2},{1,3},{2,4},{3,5},{4,6},{5,7},{6,0},{7,1},{8,10},{9,11},{10,... | collective-permute-start | bytes 2949128 | tf_op jit(solution)/shard_map/ppermute | solution.py:25
  464.5 1.3 collective-permute-start.4
  465.8 5.1 collective-permute-start.5
  468.3 3.9 collective-permute-start.6
  472.2 5.2 %collective-permute-start.7 = (f32[8192]{0:T(1024)S(1)}, f32[8192]{0:T(1024)S(1)}, u32[]{:S(2)}, u32[]{:S(2)}) collective-permute-start(f32[8192]{0:T(1024)S(1)} %maximum_maximum_fusion.1), channel_id=1, source_target_pairs={{0,16},{8,24},{16,32},{24,40},{32,48},{40,56},{48,0},{56,8},{64,80... | collective-permute-start | bytes 98312 | tf_op jit(solution)/shard_map/ppermute | solution.py:25
  477.4 3.9 collective-permute-start.8
  481.4 32.9 %copy-start = (f32[8192]{0:T(1024)}, f32[8192]{0:T(1024)S(1)}, u32[]{:S(2)}) copy-start(f32[8192]{0:T(1024)S(1)} %maximum_maximum_fusion) | copy-start | bytes 98308
  498.8 5.2 %collective-permute-start.9 = (f32[192]{0:T(256)S(1)}, f32[192]{0:T(256)S(1)}, u32[]{:S(2)}, u32[]{:S(2)}) collective-permute-start(f32[192]{0:T(256)S(1)} %fusion.1), channel_id=1, source_target_pairs={{0,1},{1,0},{2,3},{3,2},{4,5},{5,4},{6,7},{7,6},{8,9},{9,8},{10,11... | collective-permute-start | bytes 2312 | tf_op jit(solution)/shard_map/ppermute | solution.py:25
  503.9 4.9 collective-permute-start.11
  504.0 4.8 collective-permute-start.10
  508.8 4.8 collective-permute-start.12
